TPU v7x, 32 devices: a whole 2x2x4 slice. The times are simulated.
32 devices in a mesh: seq: 8 (over z, x), tp: 4 (over y, core).
Axes of the slice: x: 2, y: 2, z: 4, core: 2. Of those that a mesh axis runs over, the one named last changes fastest.
Arguments:
- queries: bfloat16 [1024, 4096], P('seq', 'tp'), may hold values from -600 to 600
- suffix_keys: bfloat16 [1024, 1024], P('seq', 'tp'), may hold values from -6 to 6
- suffix_values: bfloat16 [1024, 1024], P('seq', 'tp'), may hold values from -6 to 6
- prefix_keys: bfloat16 [512, 1024], P('seq', 'tp'), may hold values from -6 to 6
- prefix_values: bfloat16 [512, 1024], P('seq', 'tp'), may hold values from -6 to 6
- suffix_lengths: int32 [24], replicated, may hold values from 1 to 128, 1024 in all
- request_group: int32 [24], replicated, may hold values from 0 to 3
- block_group: int32 [8], replicated, may hold values from 0 to 3, as said below
Outputs:
- attended: bfloat16 [1024, 4096], P('seq', 'tp')
- cache_keys: bfloat16 [1024, 1024], P(('seq', 'tp'))
- cache_values: bfloat16 [1024, 1024], P(('seq', 'tp'))
Inputs may be any that keep to these rules, and one draw needn't show every extreme that they name: `suffix_lengths`: the suffixes fill the 1024 packed tokens end to end in order; the longest has exactly 128 tokens. `block_group`: each prefix is held by exactly 2 blocks, in any order.
All inputs are finite; a program needn't handle non-finite values.
Results may differ from a plain program's by a relative error of at most 0.009.
The roundings to bfloat16 on the way count: a program that leaves them out, or rounds other values in their place, can miss the bound.
Values may be sent and summed in bfloat16 or wider, within the bound.
No kernel may reach another device: no remote copies, remote signals or barrier semaphores. Data moves between devices by JAX's collectives and lax.ppermute only.
A program may use at most 64 MiB of HBM per device.

v0:
```python
import math
import jax
import jax.numpy as jnp
from jax import lax
from jax.sharding import PartitionSpec as P

HD = 128
GROUPS = 4
BIG_NEGATIVE = -1e30


def from_behind(array, axis, by):
    length = lax.axis_size(axis)
    pairs = [(i, i + by) for i in range(length) if 0 <= i + by < length]
    return lax.ppermute(array, axis, pairs)


def rotate(values, position):
    half = values.shape[-1] // 2
    freq = jnp.exp(
        jnp.arange(half, dtype=jnp.float32) * (-2.0 * math.log(500000.0) / values.shape[-1])
    )
    angle = position.astype(jnp.float32)[:, None] * freq[None, :]
    cosine = jnp.cos(angle)[:, None, :]
    sine = jnp.sin(angle)[:, None, :]
    floats = values.astype(jnp.float32)
    lower = floats[..., :half]
    upper = floats[..., half:]
    return jnp.concatenate(
        [lower * cosine - upper * sine, upper * cosine + lower * sine], axis=-1
    ).astype(jnp.bfloat16)


def token_info(index, suffix_lengths, request_group):
    ends = jnp.cumsum(suffix_lengths)
    request = jnp.sum((index[:, None] >= ends[None, :]).astype(jnp.int32), axis=1)
    onehot = request[:, None] == jnp.arange(suffix_lengths.shape[0], dtype=jnp.int32)[None, :]
    first = jnp.sum(jnp.where(onehot, (ends - suffix_lengths)[None, :], 0), axis=1)
    group = jnp.sum(jnp.where(onehot, request_group[None, :], 0), axis=1)
    return (request, index - first, group)


def body(
    queries,
    suffix_keys,
    suffix_values,
    prefix_keys,
    prefix_values,
    suffix_lengths,
    request_group,
    block_group,
):
    rows = queries.shape[0]
    kv_cols = suffix_keys.shape[1]
    kv_heads = kv_cols // HD
    q_heads = queries.shape[1] // HD
    repeat = q_heads // kv_heads
    devices = lax.axis_size("seq")
    me = lax.axis_index("seq")
    block_rows = prefix_keys.shape[0]
    prefix_len = block_rows * devices // GROUPS
    span = max(1, min(2048 // rows, devices // 8))
    scale = HD ** (-0.5)
    index = me * rows + jnp.arange(rows, dtype=jnp.int32)
    request, offset, group = token_info(index, suffix_lengths, request_group)
    position = offset + prefix_len
    q_rot = rotate(queries.reshape(rows, q_heads, HD), position).reshape(rows, kv_heads, repeat, HD)
    k_rot = rotate(suffix_keys.reshape(rows, kv_heads, HD), position).reshape(rows, kv_cols)

    def update(carry, keys, values, visible):
        high, total, accum = carry
        keys_split = keys.reshape(keys.shape[0], kv_heads, HD)
        values_split = values.reshape(values.shape[0], kv_heads, HD)
        scores = (
            jnp.einsum("bgrd,kgd->bgrk", q_rot, keys_split, preferred_element_type=jnp.float32)
            * scale
        )
        mask = visible[:, None, None, :]
        scores = jnp.where(mask, scores, BIG_NEGATIVE)
        new_high = jnp.maximum(high, jnp.max(scores, axis=-1))
        weights = jnp.where(mask, jnp.exp(scores - new_high[..., None]), 0.0)
        factor = jnp.exp(high - new_high)
        total = total * factor + jnp.sum(weights, axis=-1)
        accum = accum * factor[..., None] + jnp.einsum(
            "bgrk,kgd->bgrd",
            weights.astype(jnp.bfloat16),
            values_split,
            preferred_element_type=jnp.float32,
        )
        return (new_high, total, accum)

    def guarded(carry, keys, values, visible):
        return update(carry, keys, values, visible)

    def suffix_visible(back):
        key_index = (me - back) * rows + jnp.arange(rows, dtype=jnp.int32)
        key_request, _, _ = token_info(key_index, suffix_lengths, request_group)
        return (
            (key_index[None, :] >= 0)
            & (key_request[None, :] == request[:, None])
            & (key_index[None, :] <= index[:, None])
        )

    start_state = (
        jnp.full((rows, kv_heads, repeat), BIG_NEGATIVE, jnp.float32),
        jnp.zeros((rows, kv_heads, repeat), jnp.float32),
        jnp.zeros((rows, kv_heads, repeat, HD), jnp.float32),
    )
    carry = start_state
    keys = lax.all_gather(prefix_keys, "seq", axis=0, tiled=True)
    values = lax.all_gather(prefix_values, "seq", axis=0, tiled=True)
    count = keys.shape[0]
    width = 512

    def one_step(state, step):
        first = step * width
        keys_part = lax.dynamic_slice_in_dim(keys, first, width, 0)
        values_part = lax.dynamic_slice_in_dim(values, first, width, 0)
        row_index = first + jnp.arange(width, dtype=jnp.int32)
        holder = row_index // block_rows
        matches = holder[:, None] == jnp.arange(block_group.shape[0], dtype=jnp.int32)[None, :]
        row_group = jnp.sum(jnp.where(matches, block_group[None, :], 0), axis=1)
        visible = row_group[None, :] == group[:, None]
        return (guarded(state, keys_part, values_part, visible), None)

    carry, _ = lax.scan(one_step, carry, jnp.arange(count // width, dtype=jnp.int32))
    carry = guarded(carry, k_rot, suffix_values, suffix_visible(0))
    for back in range(1, span + 1):
        earlier_keys, earlier_values = from_behind((k_rot, suffix_values), "seq", back)
        carry = guarded(carry, earlier_keys, earlier_values, suffix_visible(back))
    high, total, accum = carry
    attended = (accum / total[..., None]).reshape(rows, q_heads * HD).astype(jnp.bfloat16)
    cache_keys, cache_values = (
        lax.all_to_all(k_rot, "tp", split_axis=0, concat_axis=1, tiled=True),
        lax.all_to_all(suffix_values, "tp", split_axis=0, concat_axis=1, tiled=True),
    )
    return (attended, cache_keys, cache_values)


def solution(mesh):
    return jax.shard_map(
        body,
        mesh=mesh,
        in_specs=(
            P("seq", "tp"),
            P("seq", "tp"),
            P("seq", "tp"),
            P("seq", "tp"),
            P("seq", "tp"),
            P(),
            P(),
            P(),
        ),
        out_specs=(P("seq", "tp"), P(("seq", "tp"), None), P(("seq", "tp"), None)),
        check_vma=False,
    )
```

profile of v0, /device:TPU:0, one launch (start us, length us, event | category | flops | bytes accessed | tf_op | source)
XLA Modules:
  0.0 101.6 jit_solution(3033059807300362979)
XLA Ops:
  0.7 0.8 copy.95
  2.4 0.7 select_reduce_fusion.2
  3.1 0.9 copy.101
  4.7 0.7 copy.106
  5.5 5.5 %collective-permute-start = (bf16[128,256]{0,1:T(8,128)(2,1)}, bf16[128,256]{0,1:T(8,128)(2,1)}, u32[]{:S(2)}, u32[]{:S(2)}) collective-permute-start(bf16[128,256]{0,1:T(8,128)(2,1)} %bitcast.19), channel_id=1, source_target_pairs={{0,4},{4,8},{8,12},{12,16},{16,20},{20,24},{24,28},{1,5},{5,9},{9,... | collective-permute-start | bytes 196616 | tf_op jit(solution)/shard_map/ppermute | solution.py:15
  10.9 3.5 %collective-permute-start.1 = (bf16[128,256]{1,0:T(8,128)(2,1)}, bf16[128,256]{1,0:T(8,128)(2,1)}, u32[]{:S(2)}, u32[]{:S(2)}) collective-permute-start(bf16[128,256]{1,0:T(8,128)(2,1)} %param.10), channel_id=1, source_target_pairs={{0,4},{4,8},{8,12},{12,16},{16,20},{20,24},{24,28},{1,5},{5,9},{9,... | collective-permute-start | bytes 196616 | tf_op jit(solution)/shard_map/ppermute | solution.py:15
  15.2 3.3 %all-to-all-start = ((bf16[4,32,256]{2,1,0:T(8,128)(2,1)}), bf16[4,32,256]{2,1,0:T(8,128)(2,1)S(1)}, u32[]{:S(2)}, u32[]{:S(2)}) async-start(bf16[4,32,256]{2,1,0:T(8,128)(2,1)} %convert_element_type.70), calls=%async_computation | async-start | bytes 131072 | tf_op jit(solution)/shard_map/all_to_all | solution.py:134
  18.9 31.0 %all_gather.6 = bf16[512,256]{1,0:T(8,128)(2,1)S(1)} all-gather(bf16[64,256]{1,0:T(8,128)(2,1)S(1)} %copy-done.7), channel_id=1, replica_groups=mesh['seq'=8,'tp'=4] {'seq'}, dimensions={0}, use_global_device_ids=true | all-gather | bytes 294912 | tf_op jit(solution)/shard_map/all_gather | solution.py:110
  50.4 0.8 compare_and_fusion
  51.2 1.2 %bitcast_reduce_fusion = (f32[128,2,4]{0,2,1:T(4,128)}, f32[2,128,4,512]{3,1,2,0:T(8,128)S(1)}) fusion(pred[128,512]{1,0:T(8,128)(4,1)S(1)} %broadcast_compare_fusion, bf16[512,2,128,1]{0,2,3,1:T(8,128)(2,1)S(1)} %bitcast.101, bf16[128,2,4,64]{3,0,2,1:T(8,128)(2,1)S(1)} %bitcast.98, bf16[128,2,4,64]{3,0,2,1:T(8,128)(2,1)S(1)} %bitcast.95), kind=kOutput, calls=%fused_computation.1 | convolution fusion | flops 136313856 | bytes 2691072 | tf_op jit(solution)/shard_map/while/body/eval_jaxpr/bgrd,kgd->bgrk/dot_general | solution.py:75
  52.4 0.9 fusion.49
  53.9 3.9 %all-to-all-start.1 = ((bf16[4,32,256]{2,1,0:T(8,128)(2,1)}), bf16[4,32,256]{2,1,0:T(8,128)(2,1)}, u32[]{:S(2)}, u32[]{:S(2)}) async-start(bf16[4,32,256]{2,1,0:T(8,128)(2,1)} %bitcast.29), calls=%async_computation.1 | async-start | bytes 131072 | tf_op jit(solution)/shard_map/all_to_all | solution.py:135
  57.8 31.0 %all_gather.7 = bf16[512,256]{1,0:T(8,128)(2,1)S(1)} all-gather(bf16[64,256]{1,0:T(8,128)(2,1)} %param.12), channel_id=1, replica_groups=mesh['seq'=8,'tp'=4] {'seq'}, dimensions={0}, use_global_device_ids=true | all-gather | bytes 294912 | tf_op jit(solution)/shard_map/all_gather | solution.py:111
  88.9 0.9 copy.124
  89.8 0.8 copy.100
  90.7 1.5 %copy.131 = bf16[4,4,8,256]{3,2,0,1:T(8,128)(2,1)} copy(bf16[4,4,8,256]{3,2,1,0:T(8,128)(2,1)} %bitcast.106) | data formatting | bytes 131072 | tf_op jit(solution)/shard_map/all_to_all | solution.py:134
  92.2 1.5 %copy.132 = bf16[4,4,8,256]{3,2,0,1:T(8,128)(2,1)} copy(bf16[4,4,8,256]{3,2,1,0:T(8,128)(2,1)} %bitcast.46) | data formatting | bytes 131072 | tf_op jit(solution)/shard_map/all_to_all | solution.py:135
  93.6 1.2 %fusion.48 = (f32[128,2,4]{0,2,1:T(4,128)S(1)}, f32[128,2,4,128]{0,3,2,1:T(8,128)S(1)}) fusion(bf16[128,2,128,1]{0,2,3,1:T(8,128)(2,1)} %bitcast.39, bf16[128,2,4,64]{3,0,2,1:T(8,128)(2,1)S(1)} %bitcast.100, bf16[128,2,4,64]{3,0,2,1:T(8,128)(2,1)S(1)} %bitcast.97, pred[128,128]{0,1:T(8,128)(4,1)} %get-tuple-element.67), kind=kOutput, calls=%fused_computation.88 | convolution fusion | flops 34470912 | bytes 872448 | tf_op jit(solution)/shard_map/bgrd,kgd->bgrk/dot_general | solution.py:75
  94.9 0.7 fusion.44
  96.0 0.7 fusion.2
  96.9 1.6 %fusion.7 = f32[128,2,4,128]{0,3,2,1:T(8,128)} fusion(f32[128,2,4,128]{0,3,2,1:T(8,128)S(1)} %convolution_bitcast_fusion.1, bf16[512,2,128,1]{0,2,3,1:T(8,128)(2,1)S(1)} %bitcast.104, f32[2,128,4,512]{3,1,2,0:T(8,128)S(1)} %get-tuple-element.76, f32[128,2,4]{0,2,1:T(4,128)S(1)} %get-tuple-element.66, pred[128,512]{1,0:T(8,128)(4,1)S(1)} %broadcast_compare_fusion, ...), kind=kOutput, calls=%fused_computation.13 | convolution fusion | flops 137363456 | bytes 3489792 | tf_op jit(solution)/shard_map/while/body/eval_jaxpr/bgrk,kgd->bgrd/dot_general | solution.py:84
  98.5 0.9 copy.108
  99.4 1.3 %fusion.14 = bf16[128,2,4,128]{0,3,2,1:T(8,128)(2,1)S(1)} fusion(f32[128,2,4,128]{0,3,2,1:T(8,128)} %fusion.7, bf16[128,2,128,1]{0,2,3,1:T(8,128)(2,1)S(1)} %bitcast.109, f32[128,2,4,128]{0,3,2,1:T(8,128)S(1)} %copy-done.1, f32[128,2,4]{0,2,1:T(4,128)S(1)} %get-tuple-element.52, f32[128,2,4]{0,2,1:T(4,128)S(1)} %get-tuple-element.55, ...), kind=kOutput, calls=%fused_computation.22 | convolution fusion | flops 34340864 | bytes 1400832 | tf_op jit(solution)/shard_map/bgrk,kgd->bgrd/dot_general | solution.py:84
  100.7 0.9 copy.113
  (50 shorter events, 4.4 us)
Async XLA Ops:
  0.6 17.9 %copy-start.2 = (bf16[128,1024]{1,0:T(8,128)(2,1)S(1)}, bf16[128,1024]{1,0:T(8,128)(2,1)}, u32[]{:S(2)}) copy-start(bf16[128,1024]{1,0:T(8,128)(2,1)} %param.8) | copy-start | bytes 786436
  5.5 88.2 %collective-permute-start = (bf16[128,256]{0,1:T(8,128)(2,1)}, bf16[128,256]{0,1:T(8,128)(2,1)}, u32[]{:S(2)}, u32[]{:S(2)}) collective-permute-start(bf16[128,256]{0,1:T(8,128)(2,1)} %bitcast.19), channel_id=1, source_target_pairs={{0,4},{4,8},{8,12},{12,16},{16,20},{20,24},{24,28},{1,5},{5,9},{9,... | collective-permute-start | bytes 196616 | tf_op jit(solution)/shard_map/ppermute | solution.py:15
  10.9 87.5 %collective-permute-start.1 = (bf16[128,256]{1,0:T(8,128)(2,1)}, bf16[128,256]{1,0:T(8,128)(2,1)}, u32[]{:S(2)}, u32[]{:S(2)}) collective-permute-start(bf16[128,256]{1,0:T(8,128)(2,1)} %param.10), channel_id=1, source_target_pairs={{0,4},{4,8},{8,12},{12,16},{16,20},{20,24},{24,28},{1,5},{5,9},{9,... | collective-permute-start | bytes 196616 | tf_op jit(solution)/shard_map/ppermute | solution.py:15
  14.5 4.4 %copy-start.7 = (bf16[64,256]{1,0:T(8,128)(2,1)S(1)}, bf16[64,256]{1,0:T(8,128)(2,1)}, u32[]{:S(2)}) copy-start(bf16[64,256]{1,0:T(8,128)(2,1)} %param.11) | copy-start | bytes 98308
  15.2 38.1 %all-to-all-start = ((bf16[4,32,256]{2,1,0:T(8,128)(2,1)}), bf16[4,32,256]{2,1,0:T(8,128)(2,1)S(1)}, u32[]{:S(2)}, u32[]{:S(2)}) async-start(bf16[4,32,256]{2,1,0:T(8,128)(2,1)} %convert_element_type.70), calls=%async_computation | async-start | bytes 131072 | tf_op jit(solution)/shard_map/all_to_all | solution.py:134
  18.6 31.6 %copy-start.8 = (s32[8]{0:T(128)S(1)}, s32[8]{0:T(128)}, u32[]{:S(2)}) copy-start(s32[8]{0:T(128)} %param.15) | copy-start | bytes 100
  53.3 0.6 copy-start.4
  53.9 38.2 %all-to-all-start.1 = ((bf16[4,32,256]{2,1,0:T(8,128)(2,1)}), bf16[4,32,256]{2,1,0:T(8,128)(2,1)}, u32[]{:S(2)}, u32[]{:S(2)}) async-start(bf16[4,32,256]{2,1,0:T(8,128)(2,1)} %bitcast.29), calls=%async_computation.1 | async-start | bytes 131072 | tf_op jit(solution)/shard_map/all_to_all | solution.py:135
  94.9 2.0 %copy-start = (f32[128,2,4,128]{0,3,2,1:T(8,128)}, f32[128,2,4,128]{0,3,2,1:T(8,128)S(1)}, u32[]{:S(2)}) copy-start(f32[128,2,4,128]{0,3,2,1:T(8,128)S(1)} %get-tuple-element.72) | copy-start | bytes 1572868
  94.9 1.8 %copy-start.5 = (pred[128,128]{0,1:T(8,128)(4,1)S(1)}, pred[128,128]{0,1:T(8,128)(4,1)}, u32[]{:S(2)}) copy-start(pred[128,128]{0,1:T(8,128)(4,1)} %get-tuple-element.67) | copy-start | bytes 49156
  95.7 1.1 %copy-start.6 = (f32[128,2,4]{0,2,1:T(4,128)S(1)}, f32[128,2,4]{0,2,1:T(4,128)}, u32[]{:S(2)}) copy-start(f32[128,2,4]{0,2,1:T(4,128)} %get-tuple-element.75) | copy-start | bytes 12292
  95.7 1.1 %copy-start.3 = (bf16[512,256]{0,1:T(8,128)(2,1)S(1)}, bf16[512,256]{0,1:T(8,128)(2,1)}, u32[]{:S(2)}) copy-start(bf16[512,256]{0,1:T(8,128)(2,1)} %copy.100) | copy-start | bytes 786436
  96.9 2.6 %copy-start.1 = (f32[128,2,4,128]{0,3,2,1:T(8,128)S(1)}, f32[128,2,4,128]{0,3,2,1:T(8,128)}, u32[]{:S(2)}) copy-start(f32[128,2,4,128]{0,3,2,1:T(8,128)} %copy-done) | copy-start | bytes 1572868
where the time goes:
time: 102 us
  blocking collectives  62 us (61%)
  starting transfers between devices  16.1 us (16%)
  local copies, waits for them, and re-layouts  11.1 us (11%)
  matrix products  6.46 us (6%)
  other arithmetic  5.01 us (5%)
    all_gather x1, blocking collectives, body(): values = lax.all_gather(prefix_values, 'seq', axis=0, tiled=True)  31 us
    all_gather x1, blocking collectives, body(): keys = lax.all_gather(prefix_keys, 'seq', axis=0, tiled=True)  31 us
    ppermute x2, starting transfers between devices, from_behind(): return lax.ppermute(array, axis, pairs)  8.92 us
    all_to_all x1, starting transfers between devices, body(): lax.all_to_all(suffix_values, 'tp', split_axis=0, concat_axis=1, tiled=True)  3.89 us
    dot_general x3, matrix products, update(): jnp.einsum('bgrd,kgd->bgrk', q_rot, keys_split, preferred_element_type=jn...  3.34 us
    all_to_all x1, starting transfers between devices, body(): lax.all_to_all(k_rot, 'tp', split_axis=0, concat_axis=1, tiled=True)  3.28 us
    dot_general x3, matrix products, update(): jnp.einsum('bgrk,kgd->bgrd', weights.astype(jnp.bfloat16), values_split,...  3.12 us
    unnamed x23, local copies, waits for them, and re-layouts  2.76 us
  transfers between devices with their start and end apart: 4, of which 0 were waited for; matrix products, arithmetic and copies ran while one was open for 14% of the time, Pallas kernels for 0%

commit v1 on v0

--- a/solution.py
+++ b/solution.py
@@ -3,6 +3,7 @@
 import jax.numpy as jnp
 from jax import lax
 from jax.sharding import PartitionSpec as P
+from jax.lax import all_gather
 
 HD = 128
 GROUPS = 4
@@ -107,8 +108,13 @@
         jnp.zeros((rows, kv_heads, repeat, HD), jnp.float32),
     )
     carry = start_state
-    keys = lax.all_gather(prefix_keys, "seq", axis=0, tiled=True)
-    values = lax.all_gather(prefix_values, "seq", axis=0, tiled=True)
+    keys, values = jnp.split(
+        all_gather(
+            jnp.concatenate([prefix_keys, prefix_values], 1), axis_name="seq", axis=0, tiled=True
+        ),
+        [prefix_keys.shape[1]],
+        1,
+    )
     count = keys.shape[0]
     width = 512
 

time: 102 us -> 69.8 us (0.68)
  blocking collectives: 62 us -> 31.6 us
  matrix products: 6.46 us -> 4.43 us
    all_gather x2 -> x1, blocking collectives: 62 us -> 31.6 us  [body(): all_gather(jnp.concatenate([prefix_keys, prefix_values], 1), axis_name='s...]
    dot_general x3, matrix products: 3.12 us -> 1.16 us  [update(): jnp.einsum('bgrk,kgd->bgrd', weights.astype(jnp.bfloat16), values_split,...]
    unnamed x23 -> x30, local copies, waits for them, and re-layouts: 2.76 us -> 2.29 us
  transfers between devices with their start and end apart: 4 -> 4, of which waited for: 0 -> 0; matrix products, arithmetic and copies ran while one was open for 14% -> 19% of each run, Pallas kernels for 0% -> 0%
where the time goes in v1:
time: 69.8 us; the launch traced here: 69.1 us
  blocking collectives  31.6 us (45%)
  starting transfers between devices  16.7 us (24%)
  local copies, waits for them, and re-layouts  10.5 us (15%)
  other arithmetic  4.87 us (7%)
  matrix products  4.43 us (6%)
  between operations  1.02 us (1%)
    all_gather x1, blocking collectives, body(): all_gather(jnp.concatenate([prefix_keys, prefix_values], 1), axis_name='s...  31.6 us
    ppermute x2, starting transfers between devices, from_behind(): return lax.ppermute(array, axis, pairs)  8.92 us
    all_to_all x1, starting transfers between devices, body(): lax.all_to_all(suffix_values, 'tp', split_axis=0, concat_axis=1, tiled=True)  3.9 us
    all_to_all x1, starting transfers between devices, body(): lax.all_to_all(k_rot, 'tp', split_axis=0, concat_axis=1, tiled=True)  3.89 us
    dot_general x3, matrix products, update(): jnp.einsum('bgrd,kgd->bgrk', q_rot, keys_split, preferred_element_type=jn...  3.27 us
    unnamed x30, local copies, waits for them, and re-layouts  2.29 us
    convert_element_type x3, local copies, waits for them, and re-layouts, rotate(): return jnp.concatenate([lower * cosine - upper * sine, upper * cosine + l...  1.48 us
    all_to_all x1, local copies, waits for them, and re-layouts, body(): lax.all_to_all(suffix_values, 'tp', split_axis=0, concat_axis=1, tiled=True)  1.47 us
  transfers between devices with their start and end apart: 4, of which 0 were waited for; matrix products, arithmetic and copies ran while one was open for 19% of the time, Pallas kernels for 0%

profile of v1, /device:TPU:0, one launch (start us, length us, event | category | flops | bytes accessed | tf_op | source)
XLA Modules:
  0.0 69.1 jit_solution(6173528633228958570)
XLA Ops:
  0.7 0.8 %copy.100 = s32[24,1]{1,0:T(8,128)S(1)} copy(s32[24,1]{0,1:T(1,128)} %bitcast.108) | data formatting | bytes 192 | tf_op jit(solution)/shard_map/reshape.328
  1.6 0.7 sub.87
  2.4 0.7 %select_reduce_fusion.2 = (s32[128]{0:T(128)S(1)}, s32[128]{0:T(128)S(1)}) fusion(s32[24]{0:T(128)} %param.14, s32[128]{0:T(128)S(1)} %get-tuple-element.49, s32[24]{0:T(128)S(1)} %sub.87), kind=kLoop, calls=%fused_computation.55 | loop fusion | flops 15104 | bytes 1728 | tf_op jit(solution)/shard_map/reduce_sum | solution.py:40
  3.1 0.9 %copy.107 = bf16[128,256]{0,1:T(8,128)(2,1)S(1)} copy(bf16[128,256]{1,0:T(8,128)(2,1)} %param.9) | data formatting | bytes 131072 | tf_op args[1]
  4.7 0.7 %copy.112 = bf16[128,2,128]{0,2,1:T(8,128)(2,1)} copy(bf16[128,2,128]{2,0,1:T(8,128)(2,1)S(1)} %maximum_convert_fusion) | data formatting | bytes 131072 | tf_op jit(solution)/shard_map/convert_element_type | solution.py:32
  5.5 5.5 %collective-permute-start = (bf16[128,256]{0,1:T(8,128)(2,1)}, bf16[128,256]{0,1:T(8,128)(2,1)}, u32[]{:S(2)}, u32[]{:S(2)}) collective-permute-start(bf16[128,256]{0,1:T(8,128)(2,1)} %bitcast.19), channel_id=1, source_target_pairs={{0,4},{4,8},{8,12},{12,16},{16,20},{20,24},{24,28},{1,5},{5,9},{9,... | collective-permute-start | bytes 196616 | tf_op jit(solution)/shard_map/ppermute | solution.py:16
  10.9 3.5 %collective-permute-start.1 = (bf16[128,256]{1,0:T(8,128)(2,1)}, bf16[128,256]{1,0:T(8,128)(2,1)}, u32[]{:S(2)}, u32[]{:S(2)}) collective-permute-start(bf16[128,256]{1,0:T(8,128)(2,1)} %param.10), channel_id=1, source_target_pairs={{0,4},{4,8},{8,12},{12,16},{16,20},{20,24},{24,28},{1,5},{5,9},{9,... | collective-permute-start | bytes 196616 | tf_op jit(solution)/shard_map/ppermute | solution.py:16
  14.5 0.7 convert_element_type.70
  15.2 3.9 %all-to-all-start = ((bf16[4,32,256]{2,1,0:T(8,128)(2,1)}), bf16[4,32,256]{2,1,0:T(8,128)(2,1)}, u32[]{:S(2)}, u32[]{:S(2)}) async-start(bf16[4,32,256]{2,1,0:T(8,128)(2,1)} %convert_element_type.70), calls=%async_computation | async-start | bytes 131072 | tf_op jit(solution)/shard_map/all_to_all | solution.py:140
  19.5 31.6 %all_gather.3 = bf16[512,512]{1,0:T(8,128)(2,1)S(1)} all-gather(bf16[64,512]{1,0:T(8,128)(2,1)S(1)} %pad_maximum_fusion.1), channel_id=1, replica_groups=mesh['seq'=8,'tp'=4] {'seq'}, dimensions={0}, use_global_device_ids=true | all-gather | bytes 589824 | tf_op jit(solution)/shard_map/all_gather | solution.py:112
  51.8 1.2 %fusion = (f32[128,2,4]{0,2,1:T(4,128)}, f32[2,512,128,4]{2,1,3,0:T(8,128)S(1)}) fusion(pred[128,512]{0,1:T(8,128)(4,1)S(1)} %broadcast_compare_fusion, bf16[512,2,128,1]{0,2,3,1:T(8,128)(2,1)S(1)} %bitcast.100, bf16[128,2,4,64]{3,0,2,1:T(8,128)(2,1)S(1)} %bitcast.97, bf16[128,2,4,64]{3,0,2,1:T(8,128)(2,1)S(1)} %bitcast.94), kind=kOutput, calls=%fused_computation.2 | convolution fusion | flops 136313856 | bytes 2691072 | tf_op jit(solution)/shard_map/while/body/eval_jaxpr/bgrd,kgd->bgrk/dot_general | solution.py:76
  52.9 0.8 %compare_and_fusion = (pred[128,128]{0,1:T(8,128)(4,1)}, pred[128,128]{0,1:T(8,128)(4,1)S(1)}) fusion(s32[128]{0:T(128)S(1)} %get-tuple-element.80, s32[128]{0:T(128)S(1)} %get-tuple-element.49, s32[128]{0:T(128)S(1)} %get-tuple-element.79, s32[128]{0:T(128)S(1)} %get-tuple-element.48, pred[128]{0:T(512)(128)(4,1)S(1)} %get-tuple-element.81, ...), kind=kLoop, calls=%fused_computation.49 | loop fusion | flops 131072 | bytes 35072 | tf_op jit(solution)/shard_map/and | solution.py:100
  53.7 3.9 %all-to-all-start.1 = ((bf16[4,32,256]{2,1,0:T(8,128)(2,1)}), bf16[4,32,256]{2,1,0:T(8,128)(2,1)}, u32[]{:S(2)}, u32[]{:S(2)}) async-start(bf16[4,32,256]{2,1,0:T(8,128)(2,1)} %bitcast.29), calls=%async_computation.1 | async-start | bytes 131072 | tf_op jit(solution)/shard_map/all_to_all | solution.py:141
  57.6 0.9 %fusion.48 = (f32[128,2,4]{0,2,1:T(4,128)}, f32[128,2,4,128]{0,3,2,1:T(8,128)S(1)}) fusion(bf16[128,2,4,64]{3,0,2,1:T(8,128)(2,1)S(1)} %bitcast.98, bf16[128,2,4,64]{3,0,2,1:T(8,128)(2,1)S(1)} %bitcast.95, bf16[128,2,128]{2,0,1:T(8,128)(2,1)S(1)} %maximum_convert_fusion, pred[128,128]{0,1:T(8,128)(4,1)S(1)} %get-tuple-element.70), kind=kOutput, calls=%fused_computation.88 | convolution fusion | flops 34470912 | bytes 872448 | tf_op jit(solution)/shard_map/bgrd,kgd->bgrk/dot_general | solution.py:76
  58.5 0.9 %copy.131 = bf16[128,256]{0,1:T(8,128)(2,1)S(1)} copy(bf16[128,256]{1,0:T(8,128)(2,1)} %param.10) | data formatting | bytes 131072 | tf_op jit(solution)/shard_map/reshape | solution.py:74
  59.4 0.8 %copy.105 = bf16[512,256]{0,1:T(8,128)(2,1)} copy(bf16[512,256]{1,0:T(8,128)(2,1)S(1)} %get-tuple-element.59) | data formatting | bytes 524288 | tf_op jit(solution)/shard_map/split | solution.py:111
  60.3 1.5 %copy.139 = bf16[4,4,8,256]{3,2,0,1:T(8,128)(2,1)} copy(bf16[4,4,8,256]{3,2,1,0:T(8,128)(2,1)} %bitcast.44) | data formatting | bytes 131072 | tf_op jit(solution)/shard_map/all_to_all | solution.py:140
  61.8 1.5 %copy.140 = bf16[4,4,8,256]{3,2,0,1:T(8,128)(2,1)} copy(bf16[4,4,8,256]{3,2,1,0:T(8,128)(2,1)} %bitcast.46) | data formatting | bytes 131072 | tf_op jit(solution)/shard_map/all_to_all | solution.py:141
  63.2 1.2 %fusion.47 = (f32[128,2,4]{0,2,1:T(4,128)S(1)}, f32[128,2,4,128]{0,3,2,1:T(8,128)S(1)}) fusion(bf16[128,2,128,1]{0,2,3,1:T(8,128)(2,1)} %bitcast.39, bf16[128,2,4,64]{3,0,2,1:T(8,128)(2,1)S(1)} %bitcast.99, bf16[128,2,4,64]{3,0,2,1:T(8,128)(2,1)S(1)} %bitcast.96, pred[128,128]{0,1:T(8,128)(4,1)} %get-tuple-element.69), kind=kOutput, calls=%fused_computation.87 | convolution fusion | flops 34470912 | bytes 872448 | tf_op jit(solution)/shard_map/bgrd,kgd->bgrk/dot_general | solution.py:76
  64.5 0.7 %fusion.42 = (f32[128,2,4]{0,2,1:T(4,128)S(1)}, f32[128,2,4]{0,2,1:T(4,128)S(1)}, f32[128,2,4]{0,2,1:T(4,128)S(1)}, f32[128,2,4]{0,2,1:T(4,128)S(1)}) fusion(f32[128,2,4]{0,2,1:T(4,128)S(1)} %get-tuple-element.73, f32[128,2,4]{0,2,1:T(4,128)} %get-tuple-element.75, f32[128,2,4]{0,2,1:T(4,128)} %get-tuple-element.77), kind=kLoop, calls=%fused_computation.83 | loop fusion | flops 5120 | bytes 28672 | tf_op jit(solution)/shard_map/max | solution.py:81
  65.6 0.5 fusion.1
  66.3 0.7 fusion.6
  67.0 0.9 %copy.114 = bf16[128,256]{0,1:T(8,128)(2,1)S(1)} copy(bf16[128,256]{1,0:T(8,128)(2,1)} %collective-permute-done.1) | data formatting | bytes 131072 | tf_op jit(solution)/shard_map/ppermute | solution.py:16
  68.3 0.9 %copy.119 = bf16[128,1024]{1,0:T(8,128)(2,1)} copy(bf16[128,1024]{0,1:T(8,128)(2,1)S(1)} %bitcast.104) | data formatting | bytes 524288
  (57 shorter events, 2.8 us)
Async XLA Ops:
  0.6 18.5 %copy-start.2 = (bf16[128,1024]{1,0:T(8,128)(2,1)S(1)}, bf16[128,1024]{1,0:T(8,128)(2,1)}, u32[]{:S(2)}) copy-start(bf16[128,1024]{1,0:T(8,128)(2,1)} %param.8) | copy-start | bytes 786436
  5.5 57.8 %collective-permute-start = (bf16[128,256]{0,1:T(8,128)(2,1)}, bf16[128,256]{0,1:T(8,128)(2,1)}, u32[]{:S(2)}, u32[]{:S(2)}) collective-permute-start(bf16[128,256]{0,1:T(8,128)(2,1)} %bitcast.19), channel_id=1, source_target_pairs={{0,4},{4,8},{8,12},{12,16},{16,20},{20,24},{24,28},{1,5},{5,9},{9,... | collective-permute-start | bytes 196616 | tf_op jit(solution)/shard_map/ppermute | solution.py:16
  10.9 56.1 %collective-permute-start.1 = (bf16[128,256]{1,0:T(8,128)(2,1)}, bf16[128,256]{1,0:T(8,128)(2,1)}, u32[]{:S(2)}, u32[]{:S(2)}) collective-permute-start(bf16[128,256]{1,0:T(8,128)(2,1)} %param.10), channel_id=1, source_target_pairs={{0,4},{4,8},{8,12},{12,16},{16,20},{20,24},{24,28},{1,5},{5,9},{9,... | collective-permute-start | bytes 196616 | tf_op jit(solution)/shard_map/ppermute | solution.py:16
  14.5 5.0 %copy-start.9 = (bf16[64,256]{1,0:T(8,128)(2,1)S(1)}, bf16[64,256]{1,0:T(8,128)(2,1)}, u32[]{:S(2)}) copy-start(bf16[64,256]{1,0:T(8,128)(2,1)} %param.12) | copy-start | bytes 98308
  14.5 5.0 %copy-start.10 = (bf16[64,256]{1,0:T(8,128)(2,1)S(1)}, bf16[64,256]{1,0:T(8,128)(2,1)}, u32[]{:S(2)}) copy-start(bf16[64,256]{1,0:T(8,128)(2,1)} %param.11) | copy-start | bytes 98308
  15.2 38.5 %all-to-all-start = ((bf16[4,32,256]{2,1,0:T(8,128)(2,1)}), bf16[4,32,256]{2,1,0:T(8,128)(2,1)}, u32[]{:S(2)}, u32[]{:S(2)}) async-start(bf16[4,32,256]{2,1,0:T(8,128)(2,1)} %convert_element_type.70), calls=%async_computation | async-start | bytes 131072 | tf_op jit(solution)/shard_map/all_to_all | solution.py:140
  19.5 32.0 %copy-start.11 = (s32[8]{0:T(128)S(1)}, s32[8]{0:T(128)}, u32[]{:S(2)}) copy-start(s32[8]{0:T(128)} %param.15) | copy-start | bytes 100
  53.7 8.1 %all-to-all-start.1 = ((bf16[4,32,256]{2,1,0:T(8,128)(2,1)}), bf16[4,32,256]{2,1,0:T(8,128)(2,1)}, u32[]{:S(2)}, u32[]{:S(2)}) async-start(bf16[4,32,256]{2,1,0:T(8,128)(2,1)} %bitcast.29), calls=%async_computation.1 | async-start | bytes 131072 | tf_op jit(solution)/shard_map/all_to_all | solution.py:141
  64.5 1.8 %copy-start = (f32[128,2,4,128]{0,3,2,1:T(8,128)}, f32[128,2,4,128]{0,3,2,1:T(8,128)S(1)}, u32[]{:S(2)}) copy-start(f32[128,2,4,128]{0,3,2,1:T(8,128)S(1)} %get-tuple-element.74) | copy-start | bytes 1572868
  64.5 1.7 %copy-start.4 = (pred[128,128]{0,1:T(8,128)(4,1)S(1)}, pred[128,128]{0,1:T(8,128)(4,1)}, u32[]{:S(2)}) copy-start(pred[128,128]{0,1:T(8,128)(4,1)} %get-tuple-element.69) | copy-start | bytes 49156
  65.2 1.1 %copy-start.7 = (f32[128,2,4]{0,2,1:T(4,128)}, f32[128,2,4]{0,2,1:T(4,128)S(1)}, u32[]{:S(2)}) copy-start(f32[128,2,4]{0,2,1:T(4,128)S(1)} %get-tuple-element.55) | copy-start | bytes 12292
  65.2 1.1 %copy-start.6 = (f32[128,2,4]{0,2,1:T(4,128)S(1)}, f32[128,2,4]{0,2,1:T(4,128)}, u32[]{:S(2)}) copy-start(f32[128,2,4]{0,2,1:T(4,128)} %get-tuple-element.77) | copy-start | bytes 12292
  65.2 1.1 %copy-start.3 = (bf16[512,256]{0,1:T(8,128)(2,1)S(1)}, bf16[512,256]{0,1:T(8,128)(2,1)}, u32[]{:S(2)}) copy-start(bf16[512,256]{0,1:T(8,128)(2,1)} %copy.105) | copy-start | bytes 786436
  66.3 1.7 %copy-start.1 = (f32[128,2,4,128]{0,3,2,1:T(8,128)S(1)}, f32[128,2,4,128]{0,3,2,1:T(8,128)}, u32[]{:S(2)}) copy-start(f32[128,2,4,128]{0,3,2,1:T(8,128)} %copy-done) | copy-start | bytes 1572868
  66.3 1.7 %copy-start.5 = (pred[128,128]{0,1:T(8,128)(4,1)S(1)}, pred[128,128]{0,1:T(8,128)(4,1)}, u32[]{:S(2)}) copy-start(pred[128,128]{0,1:T(8,128)(4,1)} %get-tuple-element.69) | copy-start | bytes 49156
  66.3 1.7 %copy-start.8 = (f32[128,2,4]{0,2,1:T(4,128)S(1)}, f32[128,2,4]{0,2,1:T(4,128)}, u32[]{:S(2)}) copy-start(f32[128,2,4]{0,2,1:T(4,128)} %copy-done.7) | copy-start | bytes 12292
